TPU v7x, 512 devices: a whole 4x8x8 slice. The times are simulated.
512 devices in a mesh: row: 16 (over y, core), col: 32 (over z, x).
Axes of the slice: x: 4, y: 8, z: 8, core: 2. Of those that a mesh axis runs over, the one named last changes fastest.
Arguments:
- tokens: bfloat16 [1024, 8192], P('col', 'row'), may hold values from -6 to 6
- gate_weight: bfloat16 [8192, 16384], P('row', 'col'), may hold values from -0.09375 to 0.09375
- up_weight: bfloat16 [8192, 16384], P('row', 'col'), may hold values from -0.09375 to 0.09375
- down_weight: bfloat16 [16384, 8192], P('col', 'row'), may hold values from -0.0625 to 0.0625
- gate_mask: int32 [64, 128], P('row', 'col'), may hold values from 0 to 1, as said below
- up_mask: int32 [64, 128], P('row', 'col'), may hold values from 0 to 1, as said below
- down_mask: int32 [128, 64], P('col', 'row'), may hold values from 0 to 1, as said below
Outputs:
- mixed: bfloat16 [1024, 8192], P('col', 'row')
Inputs may be any that keep to these rules, and one draw needn't show every extreme that they name: `gate_mask`: each entry is 0 or 1; the share of ones differs from one block column of hidden units to another. `up_mask`: each entry is 0 or 1; the share of ones differs from one block column of hidden units to another. `down_mask`: each entry is 0 or 1; the share of ones differs from one block row of hidden units to another.
All inputs are finite; a program needn't handle non-finite values.
Results may differ from a plain program's by a relative error of at most 0.0049.
Values may be sent and summed in bfloat16 or wider, within the bound.
No kernel may reach another device: no remote copies, remote signals or barrier semaphores. Data moves between devices by JAX's collectives and lax.ppermute only.
A program may use at most 64 MiB of HBM per device.

v0:
```python
import jax
import jax.numpy as jnp
from jax import lax
from jax.sharding import PartitionSpec as P

BLK = 128


def widen(block_mask):
    rows_blocks, cols_blocks = block_mask.shape
    spread = jnp.broadcast_to(block_mask[:, None, :, None], (rows_blocks, BLK, cols_blocks, BLK))
    return spread.reshape(rows_blocks * BLK, cols_blocks * BLK).astype(jnp.bfloat16)


def swiglu(summed, hidden_cols):
    return (jax.nn.silu(summed[:, :hidden_cols]) * summed[:, hidden_cols:]).astype(jnp.bfloat16)


def on_device(tokens, gate_weight, up_weight, down_weight, gate_mask, up_mask, down_mask):
    hidden_cols = gate_weight.shape[1]
    both_weights = jnp.concatenate(
        [gate_weight * widen(gate_mask), up_weight * widen(up_mask)], axis=1
    )
    down_eff = down_weight * widen(down_mask)
    all_tokens = lax.all_gather(tokens, "col", axis=0, tiled=True)
    summed = lax.psum_scatter(
        jnp.dot(all_tokens, both_weights, preferred_element_type=jnp.float32),
        "row",
        scatter_dimension=0,
        tiled=True,
    )
    hidden_share = swiglu(summed, hidden_cols)
    hidden = lax.all_gather(hidden_share, "row", axis=0, tiled=True)
    out_rows = tokens.shape[0]
    partial_out = jnp.dot(hidden, down_eff, preferred_element_type=jnp.float32)
    whole_out = lax.psum(partial_out, "col")
    first_row = lax.axis_index("col") * out_rows
    mixed = lax.dynamic_slice_in_dim(whole_out, first_row, out_rows, 0)
    return mixed.astype(jnp.bfloat16)


def solution(mesh):
    placed = (
        P("col", "row"),
        P("row", "col"),
        P("row", "col"),
        P("col", "row"),
        P("row", "col"),
        P("row", "col"),
        P("col", "row"),
    )
    return jax.shard_map(
        on_device, mesh=mesh, in_specs=placed, out_specs=P("col", "row"), check_vma=False
    )
```

profile of v0, /device:TPU:8, one launch (start us, length us, event | category | flops | bytes accessed | tf_op | source)
XLA Modules:
  0.0 389.6 jit_solution(954516948314816408)
XLA Ops:
  6.5 0.0 all-gather.3.cloned.1.call-start
  6.5 0.7 all-gather.3.cloned.1.call-update
  7.3 0.0 reduce-scatter.4.cloned.1.call-start
  7.3 0.7 convert_element_type.29
  8.0 0.7 convert_element_type.27
  8.7 0.2 broadcast_in_dim.7
  8.9 0.2 broadcast_in_dim.6
  9.1 1.4 bitcast_multiply_fusion.2
  10.5 87.2 %all-gather.3.cloned.1.call-done = bf16[1024,512]{1,0:T(8,128)(2,1)} async-done(((bf16[32,512]{1,0:T(8,128)(2,1)}), bf16[1024,512]{1,0:T(8,128)(2,1)}) %all-gather.3.cloned.1.call-update) | async-done | bytes 1048592 | tf_op jit(solution)/shard_map/all_gather | solution.py:25
  97.7 4.5 %convolution_bitcast_fusion = f32[1024,1024]{0,1:T(8,128)} fusion(bf16[1024,512]{1,0:T(8,128)(2,1)} %all-gather.3.cloned.1.call-done, bf16[512,512]{1,0:T(8,128)(2,1)S(1)} %get-tuple-element.5, bf16[512,512]{1,0:T(8,128)(2,1)S(1)} %get-tuple-element.6), kind=kOutput, calls=%fused_computation | convolution fusion | flops 1075838976 | bytes 6291456 | tf_op jit(solution)/shard_map/dot_general | solution.py:27
  102.2 5.4 %copy.11 = f32[1024,1024]{1,0:T(8,128)} copy(f32[1024,1024]{0,1:T(8,128)} %convolution_bitcast_fusion) | data formatting | bytes 8388608
  107.5 0.0 copy-start.1
  107.5 0.0 copy-start
  107.5 0.0 reduce-scatter.4.cloned.1.call-update
  107.6 0.0 all-gather.5.cloned.1.call-start
  107.6 59.4 %reduce-scatter.4.cloned.1.call-done = f32[64,1024]{1,0:T(8,128)} async-done(((f32[1024,1024]{1,0:T(8,128)}), f32[64,1024]{1,0:T(8,128)}) %reduce-scatter.4.cloned.1.call-update) | async-done | bytes 262160 | tf_op jit(solution)/shard_map/reduce_scatter | solution.py:26
  167.1 1.6 fusion.5
  168.7 0.0 all-gather.5.cloned.1.call-update
  168.7 0.0 copy-done.1
  168.8 43.1 %all-gather.5.cloned.1.call-done = bf16[1024,512]{1,0:T(8,128)(2,1)} async-done(((bf16[64,512]{1,0:T(8,128)(2,1)}), bf16[1024,512]{1,0:T(8,128)(2,1)}) %all-gather.5.cloned.1.call-update) | async-done | bytes 1048592 | tf_op jit(solution)/shard_map/all_gather | solution.py:33
  211.9 0.2 broadcast_in_dim.8
  212.1 0.0 copy-done
  212.1 1.9 fusion.3
  214.1 168.3 %all-reduce.1 = bf16[1024,512]{1,0:T(8,128)(2,1)S(1)} all-reduce(f32[1024,512]{1,0:T(8,128)S(1)} %fusion.3), channel_id=1, replica_groups=mesh['row'=16,'col'=32] {'col'}, use_global_device_ids=true, to_apply=%region_1.2 | all-reduce | flops 524288 | bytes 3145728 | tf_op jit(solution)/shard_map/psum | solution.py:36
  382.4 0.6 dynamic-slice_convert_fusion
  (1 shorter events, 0.0 us)
Async XLA Ops:
  6.5 91.2 %all-gather.3.cloned.1.call-start = ((), (), s32[]{:S(2)}) async-start(), calls=%async_computation.1 | async-start | bytes 1081344 | tf_op jit(solution)/shard_map/all_gather | solution.py:25
  7.3 159.8 %reduce-scatter.4.cloned.1.call-start = ((), (), s32[]{:S(2)}) async-start(), calls=%async_computation.3 | async-start | bytes 4456448 | tf_op jit(solution)/shard_map/reduce_scatter | solution.py:26
  107.5 61.2 %copy-start.1 = (s32[4,4]{1,0:T(4,128)S(1)}, s32[4,4]{1,0:T(4,128)}, u32[]{:S(2)}) copy-start(s32[4,4]{1,0:T(4,128)} %param.13) | copy-start | bytes 196
  107.5 104.6 %copy-start = (bf16[512,512]{1,0:T(8,128)(2,1)S(1)}, bf16[512,512]{1,0:T(8,128)(2,1)}, u32[]{:S(2)}) copy-start(bf16[512,512]{1,0:T(8,128)(2,1)} %param.10) | copy-start | bytes 1572868
  107.6 104.3 %all-gather.5.cloned.1.call-start = ((), (), s32[]{:S(2)}) async-start(), calls=%async_computation.2 | async-start | bytes 1114112 | tf_op jit(solution)/shard_map/all_gather | solution.py:33
Sparse Core Ops, SparseCore 0:
  10.5 87.1 all-gather.2
  107.7 59.3 reduce-scatter.3
  169.2 42.6 all-gather.4
where the time goes:
time: 390 us
  waiting for transfers between devices  191 us (49%)
  blocking collectives  168 us (43%)
  between operations  13.2 us (3%)
  local copies, waits for them, and re-layouts  6.63 us (2%)
  matrix products  6.41 us (2%)
  other arithmetic  4.37 us (1%)
    psum x1, blocking collectives, on_device(): whole_out = lax.psum(partial_out, 'col')  168 us
    all_gather x1, waiting for transfers between devices, on_device(): all_tokens = lax.all_gather(tokens, 'col', axis=0, tiled=True)  87.2 us
    reduce_scatter x1, waiting for transfers between devices, on_device(): lax.psum_scatter(jnp.dot(all_tokens, both_weights, preferred_element_type...  59.4 us
    all_gather x1, waiting for transfers between devices, on_device(): hidden = lax.all_gather(hidden_share, 'row', axis=0, tiled=True)  43.1 us
  transfers between devices with their start and end apart: 3, of which 3 were waited for; matrix products, arithmetic and copies ran while one was open for 1% of the time, Pallas kernels for 0%

commit v1 on v0

--- a/solution.py
+++ b/solution.py
@@ -1,9 +1,23 @@
+import functools
 import jax
 import jax.numpy as jnp
 from jax import lax
 from jax.sharding import PartitionSpec as P
 
 BLK = 128
+
+
+def assign_entries(here_x, dev_axis):
+    dev_n = jax.lax.psum(1, dev_axis)
+    state_now = here_x
+    for nth in [u for u in (1, 2, 4, 8, 16) if u < dev_n]:
+        high = tuple(((i, i ^ nth) for i in range(dev_n)))
+        k_now = jax.lax.ppermute(state_now, dev_axis, high)
+        state_now = state_now + k_now
+    return state_now
+
+
+_connect_rows = functools.partial(assign_entries, dev_axis="col")
 
 
 def widen(block_mask):
@@ -33,7 +47,7 @@
     hidden = lax.all_gather(hidden_share, "row", axis=0, tiled=True)
     out_rows = tokens.shape[0]
     partial_out = jnp.dot(hidden, down_eff, preferred_element_type=jnp.float32)
-    whole_out = lax.psum(partial_out, "col")
+    whole_out = _connect_rows(partial_out)
     first_row = lax.axis_index("col") * out_rows
     mixed = lax.dynamic_slice_in_dim(whole_out, first_row, out_rows, 0)
     return mixed.astype(jnp.bfloat16)

time: 390 us -> 565 us (1.45)
  the two profiles are of different devices: /device:TPU:8 before, /device:TPU:1 now
where the time goes in v1:
time: 565 us
  waiting for transfers between devices  507 us (90%)
  starting transfers between devices  23.9 us (4%)
  between operations  13.2 us (2%)
  other arithmetic  7.73 us (1%)
  matrix products  6.42 us (1%)
  local copies, waits for them, and re-layouts  6 us (1%)
    ppermute x5, waiting for transfers between devices, assign_entries(): k_now = jax.lax.ppermute(state_now, dev_axis, high)  315 us
    all_gather x1, waiting for transfers between devices, on_device(): all_tokens = lax.all_gather(tokens, 'col', axis=0, tiled=True)  82.7 us
    reduce_scatter x1, waiting for transfers between devices, on_device(): lax.psum_scatter(jnp.dot(all_tokens, both_weights, preferred_element_type...  66.2 us
    all_gather x1, waiting for transfers between devices, on_device(): hidden = lax.all_gather(hidden_share, 'row', axis=0, tiled=True)  42.4 us
    ppermute x5, starting transfers between devices, assign_entries(): k_now = jax.lax.ppermute(state_now, dev_axis, high)  23.9 us
  transfers between devices with their start and end apart: 8, of which 8 were waited for; matrix products, arithmetic and copies ran while one was open for 1% of the time, Pallas kernels for 0%

profile of v1, /device:TPU:1, one launch (start us, length us, event | category | flops | bytes accessed | tf_op | source)
XLA Modules:
  0.0 564.6 jit_solution(14110691006836552139)
XLA Ops:
  6.5 0.0 all-gather.3.cloned.1.call-start
  6.5 0.7 all-gather.3.cloned.1.call-update
  7.3 0.0 reduce-scatter.4.cloned.1.call-start
  7.3 0.7 convert_element_type.27
  8.0 0.7 convert_element_type.29
  8.7 0.2 broadcast_in_dim.6
  8.9 0.2 broadcast_in_dim.7
  9.1 1.4 bitcast_multiply_fusion.2
  10.5 82.7 %all-gather.3.cloned.1.call-done = bf16[1024,512]{1,0:T(8,128)(2,1)} async-done(((bf16[32,512]{1,0:T(8,128)(2,1)}), bf16[1024,512]{1,0:T(8,128)(2,1)}) %all-gather.3.cloned.1.call-update) | async-done | bytes 1048592 | tf_op jit(solution)/shard_map/all_gather | solution.py:39
  93.2 4.5 convolution_bitcast_fusion
  97.7 5.4 copy.11
  103.1 0.0 copy-start.1
  103.1 0.0 copy-start
  103.1 0.0 reduce-scatter.4.cloned.1.call-update
  103.1 0.0 all-gather.5.cloned.1.call-start
  103.1 66.2 %reduce-scatter.4.cloned.1.call-done = f32[64,1024]{1,0:T(8,128)} async-done(((f32[1024,1024]{1,0:T(8,128)}), f32[64,1024]{1,0:T(8,128)}) %reduce-scatter.4.cloned.1.call-update) | async-done | bytes 262160 | tf_op jit(solution)/shard_map/reduce_scatter | solution.py:40
  169.4 1.6 fusion.5
  171.0 0.0 all-gather.5.cloned.1.call-update
  171.0 0.0 copy-done.1
  171.0 42.4 %all-gather.5.cloned.1.call-done = bf16[1024,512]{1,0:T(8,128)(2,1)} async-done(((bf16[64,512]{1,0:T(8,128)(2,1)}), bf16[1024,512]{1,0:T(8,128)(2,1)}) %all-gather.5.cloned.1.call-update) | async-done | bytes 1048592 | tf_op jit(solution)/shard_map/all_gather | solution.py:47
  213.5 0.2 broadcast_in_dim.8
  213.7 0.0 copy-done
  213.7 1.9 fusion.3
  215.7 3.1 collective-permute-start
  218.8 45.7 %collective-permute-done = f32[1024,512]{1,0:T(8,128)S(1)} collective-permute-done((f32[1024,512]{1,0:T(8,128)S(1)}, f32[1024,512]{1,0:T(8,128)S(1)}, u32[]{:S(2)}, u32[]{:S(2)}) %collective-permute-start) | collective-permute-done | bytes 2097184 | tf_op jit(solution)/shard_map/ppermute | solution.py:15
  264.5 0.5 add.25
  264.9 4.6 collective-permute-start.1
  269.5 44.8 %collective-permute-done.1 = f32[1024,512]{1,0:T(8,128)S(1)} collective-permute-done((f32[1024,512]{1,0:T(8,128)S(1)}, f32[1024,512]{1,0:T(8,128)S(1)}, u32[]{:S(2)}, u32[]{:S(2)}) %collective-permute-start.1) | collective-permute-done | bytes 2097184 | tf_op jit(solution)/shard_map/ppermute | solution.py:15
  314.4 0.5 add.26
  314.9 3.3 collective-permute-start.2
  318.1 43.8 %collective-permute-done.2 = f32[1024,512]{1,0:T(8,128)S(1)} collective-permute-done((f32[1024,512]{1,0:T(8,128)S(1)}, f32[1024,512]{1,0:T(8,128)S(1)}, u32[]{:S(2)}, u32[]{:S(2)}) %collective-permute-start.2) | collective-permute-done | bytes 2097184 | tf_op jit(solution)/shard_map/ppermute | solution.py:15
  361.9 0.5 add.27
  362.4 4.3 collective-permute-start.3
  366.8 89.9 %collective-permute-done.3 = f32[1024,512]{1,0:T(8,128)S(1)} collective-permute-done((f32[1024,512]{1,0:T(8,128)S(1)}, f32[1024,512]{1,0:T(8,128)S(1)}, u32[]{:S(2)}, u32[]{:S(2)}) %collective-permute-start.3) | collective-permute-done | bytes 2097184 | tf_op jit(solution)/shard_map/ppermute | solution.py:15
  456.7 0.5 add.28
  457.2 8.6 %collective-permute-start.4 = (f32[1024,512]{1,0:T(8,128)S(1)}, f32[1024,512]{1,0:T(8,128)}, u32[]{:S(2)}, u32[]{:S(2)}) collective-permute-start(f32[1024,512]{1,0:T(8,128)S(1)} %add.28), channel_id=1, source_target_pairs={{0,16},{1,17},{2,18},{3,19},{4,20},{5,21},{6,22},{7,23},{8,24},{9,... | collective-permute-start | bytes 6291464 | tf_op jit(solution)/shard_map/ppermute | solution.py:15
  465.7 90.9 %collective-permute-done.4 = f32[1024,512]{1,0:T(8,128)} collective-permute-done((f32[1024,512]{1,0:T(8,128)S(1)}, f32[1024,512]{1,0:T(8,128)}, u32[]{:S(2)}, u32[]{:S(2)}) %collective-permute-start.4) | collective-permute-done | bytes 2097184 | tf_op jit(solution)/shard_map/ppermute | solution.py:15
  556.6 1.5 fusion.6
  (1 shorter events, 0.0 us)
Async XLA Ops:
  6.5 86.7 %all-gather.3.cloned.1.call-start = ((), (), s32[]{:S(2)}) async-start(), calls=%async_computation.1 | async-start | bytes 1081344 | tf_op jit(solution)/shard_map/all_gather | solution.py:39
  7.3 162.1 %reduce-scatter.4.cloned.1.call-start = ((), (), s32[]{:S(2)}) async-start(), calls=%async_computation.3 | async-start | bytes 4456448 | tf_op jit(solution)/shard_map/reduce_scatter | solution.py:40
  103.1 68.0 %copy-start.1 = (s32[4,4]{1,0:T(4,128)S(1)}, s32[4,4]{1,0:T(4,128)}, u32[]{:S(2)}) copy-start(s32[4,4]{1,0:T(4,128)} %param.13) | copy-start | bytes 196
  103.1 110.7 %copy-start = (bf16[512,512]{1,0:T(8,128)(2,1)S(1)}, bf16[512,512]{1,0:T(8,128)(2,1)}, u32[]{:S(2)}) copy-start(bf16[512,512]{1,0:T(8,128)(2,1)} %param.10) | copy-start | bytes 1572868
  103.1 110.4 %all-gather.5.cloned.1.call-start = ((), (), s32[]{:S(2)}) async-start(), calls=%async_computation.2 | async-start | bytes 1114112 | tf_op jit(solution)/shard_map/all_gather | solution.py:47
  215.7 48.8 %collective-permute-start = (f32[1024,512]{1,0:T(8,128)S(1)}, f32[1024,512]{1,0:T(8,128)S(1)}, u32[]{:S(2)}, u32[]{:S(2)}) collective-permute-start(f32[1024,512]{1,0:T(8,128)S(1)} %fusion.3), channel_id=1, source_target_pairs={{0,1},{1,0},{2,3},{3,2},{4,5},{5,4},{6,7},{7,6},{8,9},{9,8},{10,11... | collective-permute-start | bytes 6291464 | tf_op jit(solution)/shard_map/ppermute | solution.py:15
  264.9 49.4 %collective-permute-start.1 = (f32[1024,512]{1,0:T(8,128)S(1)}, f32[1024,512]{1,0:T(8,128)S(1)}, u32[]{:S(2)}, u32[]{:S(2)}) collective-permute-start(f32[1024,512]{1,0:T(8,128)S(1)} %add.25), channel_id=1, source_target_pairs={{0,2},{1,3},{2,0},{3,1},{4,6},{5,7},{6,4},{7,5},{8,10},{9,11},{10,... | collective-permute-start | bytes 6291464 | tf_op jit(solution)/shard_map/ppermute | solution.py:15
  314.9 47.1 %collective-permute-start.2 = (f32[1024,512]{1,0:T(8,128)S(1)}, f32[1024,512]{1,0:T(8,128)S(1)}, u32[]{:S(2)}, u32[]{:S(2)}) collective-permute-start(f32[1024,512]{1,0:T(8,128)S(1)} %add.26), channel_id=1, source_target_pairs={{0,4},{1,5},{2,6},{3,7},{4,0},{5,1},{6,2},{7,3},{8,12},{9,13},{10,... | collective-permute-start | bytes 6291464 | tf_op jit(solution)/shard_map/ppermute | solution.py:15
  362.4 94.3 %collective-permute-start.3 = (f32[1024,512]{1,0:T(8,128)S(1)}, f32[1024,512]{1,0:T(8,128)S(1)}, u32[]{:S(2)}, u32[]{:S(2)}) collective-permute-start(f32[1024,512]{1,0:T(8,128)S(1)} %add.27), channel_id=1, source_target_pairs={{0,8},{1,9},{2,10},{3,11},{4,12},{5,13},{6,14},{7,15},{8,0},{9,1},... | collective-permute-start | bytes 6291464 | tf_op jit(solution)/shard_map/ppermute | solution.py:15
  457.2 99.5 %collective-permute-start.4 = (f32[1024,512]{1,0:T(8,128)S(1)}, f32[1024,512]{1,0:T(8,128)}, u32[]{:S(2)}, u32[]{:S(2)}) collective-permute-start(f32[1024,512]{1,0:T(8,128)S(1)} %add.28), channel_id=1, source_target_pairs={{0,16},{1,17},{2,18},{3,19},{4,20},{5,21},{6,22},{7,23},{8,24},{9,... | collective-permute-start | bytes 6291464 | tf_op jit(solution)/shard_map/ppermute | solution.py:15
Sparse Core Ops, SparseCore 0:
  10.5 82.6 all-gather.2
  103.2 66.1 reduce-scatter.3
  171.5 41.9 all-gather.4
